TPU v7x, 256 devices: a whole 4x4x8 slice. The times are simulated.
256 devices in a mesh: seq: 64 (over x, z, core), tensor: 4 (over y).
Axes of the slice: x: 4, y: 4, z: 8, core: 2. Of those that a mesh axis runs over, the one named last changes fastest.
Arguments:
- hidden: bfloat16 [8192, 8192], P('seq'), may hold values from -6 to 6
- gain: bfloat16 [8192], replicated, may hold values from 0.5 to 1.5
- w_query: bfloat16 [8192, 4096], P('seq', 'tensor'), may hold values from -0.0625 to 0.0625
- q_bias: bfloat16 [4096], P('tensor'), may hold values from -3 to 3
- w_keyval: bfloat16 [8192, 2, 512], P('seq', None, 'tensor'), may hold values from -0.125 to 0.125
- kv_bias: bfloat16 [2, 512], P(None, 'tensor'), may hold values from -3 to 3
- prefix_keys: bfloat16 [2, 4096, 4, 128], P(None, 'seq', 'tensor'), may hold values from -128 to 128, as said below
- prefix_values: bfloat16 [2, 4096, 4, 128], P(None, 'seq', 'tensor'), may hold values from -6 to 6
- lengths: int32 [32], replicated, may hold values from 1 to 384, 8192 in all
- assignment: int32 [32], replicated, may hold values from 0 to 1
Outputs:
- attention: bfloat16 [8192, 4096], P('seq', 'tensor')
- suffix_keys: bfloat16 [8192, 4, 128], P('seq', 'tensor')
- suffix_values: bfloat16 [8192, 4, 128], P('seq', 'tensor')
Inputs may be any that keep to these rules, and one draw needn't show every extreme that they name: Request r occupies the next lengths[r] rows of the token arrays, in order; the lengths sum to 8192 and the largest is 384. `assignment`: the prefix that request r continues. `prefix_keys`: cached keys, already rotated to positions 0 to 4095.
All inputs are finite; a program needn't handle non-finite values.
Results may differ from a plain program's by a relative error of at most 0.01.
The roundings to bfloat16 on the way count: a program that leaves them out, or rounds other values in their place, can miss the bound.
Values may be sent and summed in bfloat16 or wider, within the bound.
No kernel may reach another device: no remote copies, remote signals or barrier semaphores. Data moves between devices by JAX's collectives and lax.ppermute only.
A program may use at most 128 MiB of HBM per device.

v0:
```python
import math
import jax
import jax.numpy as jnp
from jax import lax
from jax.sharding import PartitionSpec as P

EPS = 1e-06
THETA = 1000000.0


def from_behind(shard, axis, by):
    size = lax.axis_size(axis)
    pairs = [(i, i + by) for i in range(size) if 0 <= i + by < size]
    return lax.ppermute(shard, axis, pairs)


def row_tables(lengths, assignment, all_rows):
    request_end = jnp.cumsum(lengths)
    request_start = request_end - lengths
    row_ids = jnp.arange(all_rows, dtype=jnp.int32)
    segment = jnp.sum((row_ids[:, None] >= request_end[None, :]).astype(jnp.int32), axis=1)
    request_ids = jnp.arange(lengths.shape[0], dtype=jnp.int32)
    onehot = (segment[:, None] == request_ids[None, :]).astype(jnp.int32)
    offset = row_ids - jnp.sum(onehot * request_start[None, :], axis=1)
    prefix = jnp.sum(onehot * assignment[None, :], axis=1)
    return (segment, offset, prefix)


def rotate(values, positions):
    head_size = values.shape[-1]
    half_dim = head_size // 2
    frequency = THETA ** (-2.0 * jnp.arange(half_dim, dtype=jnp.float32) / head_size)
    angles = positions.astype(jnp.float32)[:, None] * frequency[None, :]
    cosine = jnp.concatenate([jnp.cos(angles), jnp.cos(angles)], axis=-1)[:, None, :]
    sine_part = jnp.concatenate([jnp.sin(angles), jnp.sin(angles)], axis=-1)[:, None, :]
    turned = jnp.concatenate([-values[..., half_dim:], values[..., :half_dim]], axis=-1)
    return values * cosine + turned * sine_part


def local(
    hidden,
    gain,
    w_query,
    q_bias,
    w_keyval,
    kv_bias,
    prefix_keys,
    prefix_values,
    lengths,
    assignment,
):
    row_count = hidden.shape[0]
    seq_count = lax.axis_size("seq")
    seq_index = lax.axis_index("seq")
    all_rows = row_count * seq_count
    head_dim = prefix_keys.shape[3]
    kv_local = prefix_keys.shape[2]
    prefix_count = prefix_keys.shape[0]
    query_width = w_query.shape[1]
    heads_local = query_width // head_dim
    group_size = heads_local // kv_local
    pair_width = w_keyval.shape[1] * w_keyval.shape[2]
    key_width = pair_width // 2
    cache_length = prefix_keys.shape[1] * seq_count
    score_scale = head_dim ** (-0.5)
    first_row = seq_index * row_count
    prefix_ids = jnp.arange(prefix_count, dtype=jnp.int32)
    hidden_f = hidden.astype(jnp.float32)
    normed = (
        hidden_f
        * lax.rsqrt(jnp.mean(hidden_f * hidden_f, axis=1, keepdims=True) + EPS)
        * gain.astype(jnp.float32)
    ).astype(jnp.bfloat16)
    segment, offset, prefix = row_tables(lengths, assignment, all_rows)
    positions = offset + cache_length
    own_positions = lax.dynamic_slice_in_dim(positions, first_row, row_count)
    own_segment = lax.dynamic_slice_in_dim(segment, first_row, row_count)
    own_prefix = lax.dynamic_slice_in_dim(prefix, first_row, row_count)
    w_pairs = w_keyval.reshape(w_keyval.shape[0], pair_width)
    combined = jnp.concatenate([w_query, w_pairs], axis=1)
    summed = jnp.dot(
        normed,
        lax.all_gather(combined, "seq", axis=0, tiled=True),
        preferred_element_type=jnp.float32,
    )
    query_own = summed[:, :query_width] + q_bias.astype(jnp.float32)
    pairs_own = summed[:, query_width:] + kv_bias.reshape(pair_width).astype(jnp.float32)
    own_queries = rotate(query_own.reshape(row_count, heads_local, head_dim), own_positions).astype(
        jnp.bfloat16
    )
    own_keys = rotate(
        pairs_own[:, :key_width].reshape(row_count, kv_local, head_dim), own_positions
    ).astype(jnp.bfloat16)
    own_values = (
        pairs_own[:, key_width:].reshape(row_count, kv_local, head_dim).astype(jnp.bfloat16)
    )
    own_blocks = own_queries.reshape(row_count, kv_local, group_size, head_dim)
    allowed_own = (own_prefix[:, None] == prefix_ids[None, :])[:, None, None, :, None]
    initial = (
        jnp.full((row_count, kv_local, group_size), -jnp.inf, jnp.float32),
        jnp.zeros((row_count, kv_local, group_size), jnp.float32),
        jnp.zeros((row_count, kv_local, group_size, head_dim), jnp.float32),
    )
    keys_piece = lax.all_gather(prefix_keys, "seq", axis=1, tiled=True)
    values_piece = lax.all_gather(prefix_values, "seq", axis=1, tiled=True)
    piece_len = keys_piece.shape[1]
    step_rows = math.gcd(piece_len, 512)

    def inner(state, block_index):
        run_top, run_mass, run_acc = state
        key_block = lax.dynamic_slice_in_dim(keys_piece, block_index * step_rows, step_rows, 1)
        value_block = lax.dynamic_slice_in_dim(values_piece, block_index * step_rows, step_rows, 1)
        scores = (
            jnp.einsum(
                "bgqd,plgd->bgqpl", own_blocks, key_block, preferred_element_type=jnp.float32
            )
            * score_scale
        )
        scores = jnp.where(allowed_own, scores, -jnp.inf)
        new_top = jnp.maximum(run_top, jnp.max(scores, axis=(3, 4)))
        keep_share = jnp.exp(run_top - new_top)
        weights = jnp.exp(scores - new_top[..., None, None])
        new_mass = run_mass * keep_share + jnp.sum(weights, axis=(3, 4))
        new_acc = run_acc * keep_share[..., None] + jnp.einsum(
            "bgqpl,plgd->bgqd",
            weights.astype(jnp.bfloat16),
            value_block,
            preferred_element_type=jnp.float32,
        )
        return ((new_top, new_mass, new_acc), None)

    result, unused = lax.scan(inner, initial, jnp.arange(piece_len // step_rows, dtype=jnp.int32))
    fold_top, fold_mass, fold_acc = result
    prefix_top = fold_top.reshape(row_count, heads_local)
    prefix_mass = fold_mass.reshape(row_count, heads_local)
    prefix_acc = fold_acc.reshape(row_count, heads_local, head_dim)
    pair_rows = jnp.concatenate(
        [own_keys.reshape(row_count, key_width), own_values.reshape(row_count, key_width)], axis=1
    )
    depth = min(3, seq_count - 1)
    earlier = []
    for distance in range(depth, 0, -1):
        earlier.append(from_behind(pair_rows, "seq", distance))
    near_rows = jnp.concatenate(earlier + [pair_rows], axis=0)
    near_index = (
        first_row - depth * row_count + jnp.arange((depth + 1) * row_count, dtype=jnp.int32)
    )
    near_keys = near_rows[:, :key_width].reshape(near_rows.shape[0], kv_local, head_dim)
    near_values = near_rows[:, key_width:].reshape(near_rows.shape[0], kv_local, head_dim)
    near_segment = segment[jnp.clip(near_index, 0, all_rows - 1)]
    own_rows = first_row + jnp.arange(row_count, dtype=jnp.int32)
    visible = (
        (near_index[None, :] >= 0)
        & (near_segment[None, :] == own_segment[:, None])
        & (near_index[None, :] <= own_rows[:, None])
    )
    scores = (
        jnp.einsum("bgqd,ngd->bgqn", own_blocks, near_keys, preferred_element_type=jnp.float32)
        * score_scale
    )
    scores = jnp.where(visible[:, None, None, :], scores, -jnp.inf)
    local_top = jnp.max(scores, axis=3)
    weights = jnp.exp(scores - local_top[..., None])
    local_mass = jnp.sum(weights, axis=3).reshape(row_count, heads_local)
    local_acc = jnp.einsum(
        "bgqn,ngd->bgqd",
        weights.astype(jnp.bfloat16),
        near_values,
        preferred_element_type=jnp.float32,
    ).reshape(row_count, heads_local, head_dim)
    local_top = local_top.reshape(row_count, heads_local)
    joint_top = jnp.maximum(prefix_top, local_top)
    far_scale = jnp.exp(prefix_top - joint_top)
    near_scale = jnp.exp(local_top - joint_top)
    numerator = prefix_acc * far_scale[..., None] + local_acc * near_scale[..., None]
    denominator = prefix_mass * far_scale + local_mass * near_scale
    attention = (
        (numerator / denominator[..., None]).astype(jnp.bfloat16).reshape(row_count, query_width)
    )
    return (attention, own_keys, own_values)


def solution(mesh):
    in_specs = (
        P("seq", None),
        P(),
        P("seq", "tensor"),
        P("tensor"),
        P("seq", None, "tensor"),
        P(None, "tensor"),
        P(None, "seq", "tensor", None),
        P(None, "seq", "tensor", None),
        P(),
        P(),
    )
    out_specs = (P("seq", "tensor"), P("seq", "tensor", None), P("seq", "tensor", None))
    return jax.shard_map(local, mesh=mesh, in_specs=in_specs, out_specs=out_specs, check_vma=False)
```

profile of v0, /device:TPU:1, one launch (start us, length us, event | category | flops | bytes accessed | tf_op | source)
XLA Modules:
  0.0 376.9 jit_solution(10367872859374238164)
XLA Ops:
  17.5 3.1 gather_fusion
  22.4 102.5 %all-gather.6.cloned.1.call-done = bf16[8192,1280]{1,0:T(8,128)(2,1)} async-done(((bf16[128,1280]{1,0:T(8,128)(2,1)}), bf16[8192,1280]{1,0:T(8,128)(2,1)}) %all-gather.6.cloned.1.call-update) | async-done | bytes 20971536 | tf_op jit(solution)/shard_map/all_gather | solution.py:83
  124.9 9.9 %fusion.27 = f32[128,1280]{1,0:T(8,128)S(1)} fusion(bf16[8192,1280]{1,0:T(8,128)(2,1)} %all-gather.6.cloned.1.call-done, bf16[128,8192]{1,0:T(8,128)(2,1)S(1)} %copy-done.1, f32[8192]{0:T(1024)S(1)} %convert_element_type.68, f32[128]{0:T(128)} %add_rsqrt_fusion), kind=kOutput, calls=%fused_computation.33 | convolution fusion | flops 2688548864 | bytes 23757312 | tf_op jit(solution)/shard_map/dot_general | solution.py:81
  135.2 3.1 collective-permute-start
  138.2 4.4 %collective-permute-start.1 = (bf16[128,256]{1,0:T(8,128)(2,1)S(1)}, bf16[128,256]{1,0:T(8,128)(2,1)}, u32[]{:S(2)}, u32[]{:S(2)}) collective-permute-start(bf16[128,256]{1,0:T(8,128)(2,1)S(1)} %pad_maximum_fusion.3), channel_id=1, source_target_pairs={{0,8},{4,12},{8,16},{12,20},{16,24},{20,28},{24,32},{28,36},{32,40... | collective-permute-start | bytes 196616 | tf_op jit(solution)/shard_map/ppermute | solution.py:14
  145.8 56.8 %all-gather.8.cloned.1.call-done = bf16[2,4096,1,128]{3,0,2,1:T(2,128)(2,1)} async-done(((bf16[2,64,1,128]{3,0,2,1:T(2,128)(2,1)}), bf16[2,4096,1,128]{3,0,2,1:T(2,128)(2,1)}) %all-gather.8.cloned.1.call-update) | async-done | bytes 2097168 | tf_op jit(solution)/shard_map/all_gather | solution.py:105
  202.6 77.8 %all-gather.4.cloned.1.call-done = bf16[2,4096,1,128]{3,1,0,2:T(8,128)(2,1)} async-done(((bf16[2,64,1,128]{3,1,0,2:T(8,128)(2,1)}), bf16[2,4096,1,128]{3,1,0,2:T(8,128)(2,1)}) %all-gather.4.cloned.1.call-update) | async-done | bytes 2097168 | tf_op jit(solution)/shard_map/all_gather | solution.py:104
  280.4 84.7 %while.15 = (s32[]{:T(128)}, f32[128,1,8]{0,2,1:T(8,128)S(1)}, f32[128,1,8]{0,2,1:T(8,128)S(1)}, f32[128,1,8,128]{0,3,2,1:T(8,128)S(1)}, s32[8]{0:T(128)S(1)}, /...) while((s32[]{:T(128)}, f32[128,1,8]{0,2,1:T(8,128)S(1)}, ...), condition=%wide.region_8.9_spmd.clone, body=%wide.region_5.8_spmd.clone.sunk | while | flops 548804864 | bytes 32311012 | solution.py:132
  281.6 3.6 fusion.76
  286.5 3.5 fusion.79
  292.2 3.6 fusion.76
  297.1 3.5 fusion.79
  302.8 3.6 fusion.76
  307.7 3.5 fusion.79
  313.4 3.6 fusion.76
  318.3 3.5 fusion.79
  323.9 3.6 fusion.76
  328.9 3.5 fusion.79
  334.5 3.6 fusion.76
  339.5 3.5 fusion.79
  345.1 3.6 fusion.76
  350.1 3.5 fusion.79
  355.7 3.6 fusion.76
  360.6 3.5 fusion.79
  (158 shorter events, 42.5 us)
Async XLA Ops:
  7.2 117.8 %copy-start.1 = (bf16[128,8192]{1,0:T(8,128)(2,1)S(1)}, bf16[128,8192]{1,0:T(8,128)(2,1)}, u32[]{:S(2)}) copy-start(bf16[128,8192]{1,0:T(8,128)(2,1)} %param.12) | copy-start | bytes 6291460
  7.2 13.5 %copy-start.3 = (bf16[1024]{0:T(1024)(128)(2,1)S(1)}, bf16[1024]{0:T(1024)(128)(2,1)}, u32[]{:S(2)}) copy-start(bf16[1024]{0:T(1024)(128)(2,1)} %param.15) | copy-start | bytes 6148
  7.2 13.5 %copy-start.4 = (s32[32]{0:T(128)S(1)}, s32[32]{0:T(128)}, u32[]{:S(2)}) copy-start(s32[32]{0:T(128)} %param.21) | copy-start | bytes 388
  7.2 14.6 %copy-start.5 = (bf16[2,128]{1,0:T(2,128)(2,1)S(1)}, bf16[2,128]{1,0:T(2,128)(2,1)}, u32[]{:S(2)}) copy-start(bf16[2,128]{1,0:T(2,128)(2,1)} %param.17) | copy-start | bytes 1540
  7.2 117.7 %all-gather.6.cloned.1.call-start = ((), (), s32[]{:S(2)}) async-start(), calls=%async_computation.1 | async-start | bytes 21299200 | tf_op jit(solution)/shard_map/all_gather | solution.py:83
  10.0 192.6 %all-gather.8.cloned.1.call-start = ((), (), s32[]{:S(2)}) async-start(), calls=%async_computation.2 | async-start | bytes 2129920 | tf_op jit(solution)/shard_map/all_gather | solution.py:105
  11.5 268.9 %all-gather.4.cloned.1.call-start = ((), (), s32[]{:S(2)}) async-start(), calls=%async_computation | async-start | bytes 2129920 | tf_op jit(solution)/shard_map/all_gather | solution.py:104
  135.1 230.8 %copy-start.2 = (bf16[128,128]{1,0:T(8,128)(2,1)}, bf16[128,128]{1,0:T(8,128)(2,1)S(1)}, u32[]{:S(2)}) copy-start(bf16[128,128]{1,0:T(8,128)(2,1)S(1)} %get-tuple-element.139) | copy-start | bytes 98308
  135.2 230.7 %collective-permute-start = (bf16[128,256]{1,0:T(8,128)(2,1)S(1)}, bf16[128,256]{1,0:T(8,128)(2,1)}, u32[]{:S(2)}, u32[]{:S(2)}) collective-permute-start(bf16[128,256]{1,0:T(8,128)(2,1)S(1)} %pad_maximum_fusion.3), channel_id=1, source_target_pairs={{0,12},{4,16},{8,20},{12,24},{16,28},{20,32},{24,36},{28,40},{32,4... | collective-permute-start | bytes 196616 | tf_op jit(solution)/shard_map/ppermute | solution.py:14
  138.2 227.6 %collective-permute-start.1 = (bf16[128,256]{1,0:T(8,128)(2,1)S(1)}, bf16[128,256]{1,0:T(8,128)(2,1)}, u32[]{:S(2)}, u32[]{:S(2)}) collective-permute-start(bf16[128,256]{1,0:T(8,128)(2,1)S(1)} %pad_maximum_fusion.3), channel_id=1, source_target_pairs={{0,8},{4,12},{8,16},{12,20},{16,24},{20,28},{24,32},{28,36},{32,40... | collective-permute-start | bytes 196616 | tf_op jit(solution)/shard_map/ppermute | solution.py:14
  142.7 223.2 %collective-permute-start.2 = (bf16[128,256]{1,0:T(8,128)(2,1)S(1)}, bf16[128,256]{1,0:T(8,128)(2,1)}, u32[]{:S(2)}, u32[]{:S(2)}) collective-permute-start(bf16[128,256]{1,0:T(8,128)(2,1)S(1)} %pad_maximum_fusion.3), channel_id=1, source_target_pairs={{0,4},{4,8},{8,12},{12,16},{16,20},{20,24},{24,28},{28,32},{32,36}... | collective-permute-start | bytes 196616 | tf_op jit(solution)/shard_map/ppermute | solution.py:14
  144.9 135.4 %copy-start.6 = (s32[128]{0:T(128)S(1)}, s32[128]{0:T(128)}, u32[]{:S(2)}) copy-start(s32[128]{0:T(128)} %dynamic_slice.19) | copy-start | bytes 1540
  286.5 3.5 copy-start
  297.1 3.5 copy-start
  307.7 3.5 copy-start
  318.3 3.5 copy-start
  328.9 3.5 copy-start
  339.5 3.5 copy-start
  350.0 3.5 copy-start
  360.6 3.5 copy-start
Sparse Core Ops, SparseCore 0:
  10.8 114.1 all-gather.5
  128.3 74.2 all-gather.7
  205.4 74.8 all-gather.3
where the time goes:
time: 378 us; the launch traced here: 377 us
  waiting for transfers between devices  238 us (63%)
  matrix products  67.8 us (18%)
  local copies, waits for them, and re-layouts  24.4 us (6%)
  other arithmetic  17.2 us (5%)
  between operations  14.1 us (4%)
  starting transfers between devices  9.81 us (3%)
  loops' own time  5.83 us (2%)
    all_gather x1, waiting for transfers between devices, local(): lax.all_gather(combined, 'seq', axis=0, tiled=True)  103 us
    all_gather x1, waiting for transfers between devices, local(): keys_piece = lax.all_gather(prefix_keys, 'seq', axis=1, tiled=True)  77.8 us
    all_gather x1, waiting for transfers between devices, local(): values_piece = lax.all_gather(prefix_values, 'seq', axis=1, tiled=True)  56.8 us
    dot_general x8, matrix products, inner(): jnp.einsum('bgqd,plgd->bgqpl', own_blocks, key_block, preferred_element_t...  28.9 us
    dot_general x8, matrix products, inner(): jnp.einsum('bgqpl,plgd->bgqd', weights.astype(jnp.bfloat16), value_block,...  27.9 us
    dynamic_slice x16, local copies, waits for them, and re-layouts, inner(): lax.dynamic_slice_in_dim(values_piece, block_index * step_rows, step_rows...  10.4 us
    dot_general x1, matrix products, local(): jnp.dot(normed, lax.all_gather(combined, 'seq', axis=0, tiled=True), pref...  9.93 us
    ppermute x3, starting transfers between devices, from_behind(): return lax.ppermute(shard, axis, pairs)  9.69 us
  transfers between devices with their start and end apart: 6, of which 3 were waited for; matrix products, arithmetic and copies ran while one was open for 27% of the time, Pallas kernels for 0%

commit v1 on v0

--- a/solution.py
+++ b/solution.py
@@ -102,7 +102,8 @@
         jnp.zeros((row_count, kv_local, group_size, head_dim), jnp.float32),
     )
     keys_piece = lax.all_gather(prefix_keys, "seq", axis=1, tiled=True)
-    values_piece = lax.all_gather(prefix_values, "seq", axis=1, tiled=True)
+    sent = jnp.stack([prefix_values] * lax.axis_size("seq"))
+    values_piece = jnp.concatenate(lax.all_to_all(sent, "seq", 0, 0), axis=1)
     piece_len = keys_piece.shape[1]
     step_rows = math.gcd(piece_len, 512)
 

time: 378 us -> 311 us (0.82)
  waiting for transfers between devices: 238 us -> 167 us
  starting transfers between devices: 9.81 us -> 23 us
  local copies, waits for them, and re-layouts: 24.4 us -> 17.2 us
    all_to_all x0 -> x1, waiting for transfers between devices: none -> 57.1 us  [local(): values_piece = jnp.concatenate(lax.all_to_all(sent, 'seq', 0, 0), axis=1)]
    all_gather x1 -> x0, waiting for transfers between devices: 56.8 us -> none  [local(): values_piece = lax.all_gather(prefix_values, 'seq', axis=1, tiled=True)]
    all_gather x1, waiting for transfers between devices: 103 us -> 53.1 us  [local(): lax.all_gather(combined, 'seq', axis=0, tiled=True)]
    all_gather x1, waiting for transfers between devices: 77.8 us -> 56.3 us  [local(): keys_piece = lax.all_gather(prefix_keys, 'seq', axis=1, tiled=True)]
    all_to_all x0 -> x1, starting transfers between devices: none -> 13.3 us  [local(): values_piece = jnp.concatenate(lax.all_to_all(sent, 'seq', 0, 0), axis=1)]
    dynamic_slice x16 -> x0, local copies, waits for them, and re-layouts: 10.4 us -> none  [inner(): lax.dynamic_slice_in_dim(values_piece, block_index * step_rows, step_rows...]
  transfers between devices with their start and end apart: 6 -> 6, of which waited for: 3 -> 3; matrix products, arithmetic and copies ran while one was open for 27% -> 30% of each run, Pallas kernels for 0% -> 0%
where the time goes in v1:
time: 311 us; the launch traced here: 310 us
  waiting for transfers between devices  167 us (54%)
  matrix products  68.6 us (22%)
  starting transfers between devices  23 us (7%)
  local copies, waits for them, and re-layouts  17.2 us (6%)
  between operations  14.4 us (5%)
  other arithmetic  13.6 us (4%)
  loops' own time  5.71 us (2%)
    all_to_all x1, waiting for transfers between devices, local(): values_piece = jnp.concatenate(lax.all_to_all(sent, 'seq', 0, 0), axis=1)  57.1 us
    all_gather x1, waiting for transfers between devices, local(): keys_piece = lax.all_gather(prefix_keys, 'seq', axis=1, tiled=True)  56.3 us
    all_gather x1, waiting for transfers between devices, local(): lax.all_gather(combined, 'seq', axis=0, tiled=True)  53.1 us
    dot_general x8, matrix products, inner(): jnp.einsum('bgqd,plgd->bgqpl', own_blocks, key_block, preferred_element_t...  28.8 us
    dot_general x8, matrix products, inner(): jnp.einsum('bgqpl,plgd->bgqd', weights.astype(jnp.bfloat16), value_block,...  28.7 us
    all_to_all x1, starting transfers between devices, local(): values_piece = jnp.concatenate(lax.all_to_all(sent, 'seq', 0, 0), axis=1)  13.3 us
    dot_general x1, matrix products, local(): jnp.dot(normed, lax.all_gather(combined, 'seq', axis=0, tiled=True), pref...  9.91 us
    ppermute x3, starting transfers between devices, from_behind(): return lax.ppermute(shard, axis, pairs)  9.67 us
  transfers between devices with their start and end apart: 6, of which 3 were waited for; matrix products, arithmetic and copies ran while one was open for 30% of the time, Pallas kernels for 0%

profile of v1, /device:TPU:1, one launch (start us, length us, event | category | flops | bytes accessed | tf_op | source)
XLA Modules:
  0.0 309.8 jit_solution(15663743792454619223)
XLA Ops:
  12.6 13.3 %all-to-all-start = ((bf16[64,2,64,1,128]{4,2,1,3,0:T(8,128)(2,1)}), bf16[64,2,64,1,128]{4,2,1,3,0:T(8,128)(2,1)}, u32[]{:S(2)}, u32[]{:S(2)}) async-start(bf16[64,2,64,1,128]{4,2,1,3,0:T(8,128)(2,1)} %stack.2), calls=%async_computation | async-start | bytes 4194304 | tf_op jit(solution)/shard_map/all_to_all | solution.py:106
  27.4 3.1 %gather_fusion = s32[512]{0:T(512)S(1)} fusion(s32[8192]{0:T(1024)S(1)} %convert_reduce_fusion, s32[1024]{0:T(1024)S(1)} %pad_clamp_fusion), kind=kCustom, calls=%fused_computation | custom fusion | bytes 6144 | tf_op jit(solution)/shard_map/gather | solution.py:151
  32.3 57.1 %all-to-all-done = bf16[64,2,64,1,128]{4,2,1,3,0:T(8,128)(2,1)} async-done(((bf16[64,2,64,1,128]{4,2,1,3,0:T(8,128)(2,1)}), bf16[64,2,64,1,128]{4,2,1,3,0:T(8,128)(2,1)}, u32[]{:S(2)}, u32[]{:S(2)}) %all-to-all-start) | async-done | bytes 2097184 | tf_op jit(solution)/shard_map/all_to_all | solution.py:106
  92.5 53.1 %all-gather.5.cloned.1.call-done = bf16[8192,1280]{1,0:T(8,128)(2,1)} async-done(((bf16[128,1280]{1,0:T(8,128)(2,1)}), bf16[8192,1280]{1,0:T(8,128)(2,1)}) %all-gather.5.cloned.1.call-update) | async-done | bytes 20971536 | tf_op jit(solution)/shard_map/all_gather | solution.py:83
  145.6 9.9 %fusion.29 = f32[128,1280]{1,0:T(8,128)S(1)} fusion(bf16[8192,1280]{1,0:T(8,128)(2,1)} %all-gather.5.cloned.1.call-done, bf16[128,8192]{1,0:T(8,128)(2,1)S(1)} %copy-done.1, f32[8192]{0:T(1024)S(1)} %convert_element_type.68, f32[128]{0:T(128)S(1)} %add_rsqrt_fusion), kind=kOutput, calls=%fused_computation.34 | convolution fusion | flops 2688548864 | bytes 23757312 | tf_op jit(solution)/shard_map/dot_general | solution.py:81
  158.3 5.0 %collective-permute-start.1 = (bf16[128,256]{1,0:T(8,128)(2,1)S(1)}, bf16[128,256]{1,0:T(8,128)(2,1)}, u32[]{:S(2)}, u32[]{:S(2)}) collective-permute-start(bf16[128,256]{1,0:T(8,128)(2,1)S(1)} %pad_maximum_fusion.3), channel_id=1, source_target_pairs={{0,8},{4,12},{8,16},{12,20},{16,24},{20,28},{24,32},{28,36},{32,40... | collective-permute-start | bytes 196616 | tf_op jit(solution)/shard_map/ppermute | solution.py:14
  166.5 56.3 %all-gather.3.cloned.1.call-done = bf16[2,4096,1,128]{3,1,0,2:T(8,128)(2,1)} async-done(((bf16[2,64,1,128]{3,1,0,2:T(8,128)(2,1)}), bf16[2,4096,1,128]{3,1,0,2:T(8,128)(2,1)}) %all-gather.3.cloned.1.call-update) | async-done | bytes 2097168 | tf_op jit(solution)/shard_map/all_gather | solution.py:104
  222.8 74.9 %while.15 = (s32[]{:T(128)}, f32[128,1,8]{0,2,1:T(8,128)S(1)}, f32[128,1,8]{0,2,1:T(8,128)S(1)}, f32[128,1,8,128]{0,3,2,1:T(8,128)S(1)}, s32[8]{0:T(128)S(1)}, /...) while((s32[]{:T(128)}, f32[128,1,8]{0,2,1:T(8,128)S(1)}, ...), condition=%wide.region_8.9_spmd.clone, body=%wide.region_5.8_spmd.clone.sunk | while | flops 548804864 | bytes 31262436 | solution.py:133
  224.0 3.6 %fusion.78 = (f32[128,8]{0,1:T(8,128)S(1)}, f32[2,512,128,8]{2,1,3,0:T(8,128)}) fusion(pred[128,2]{0,1:T(4,128)(4,1)S(1)} %compare_bitcast_fusion.2, bf16[128,1,8,128]{3,0,2,1:T(8,128)(2,1)S(1)} %get-tuple-element.254, bf16[2,4096,1,128]{3,1,0,2:T(8,128)(2,1)} %get-tuple-element.253, s32[]{:T(128)S(6)} %select_n.55), kind=kOutput, calls=%fused_computation.6.clone.1 | convolution fusion | flops 271580160 | bytes 4722948 | tf_op jit(solution)/shard_map/while/body/eval_jaxpr/bgqd,plgd->bgqpl/dot_general | solution.py:115
  227.6 3.6 %fusion.81 = f32[128,1,8,128]{0,3,2,1:T(8,128)S(1)} fusion(f32[2,512,128,8]{2,1,3,0:T(8,128)} %get-tuple-element.220, f32[128,8]{0,1:T(8,128)S(1)} %bitcast.213, pred[128,2]{0,1:T(4,128)(4,1)S(1)} %compare_bitcast_fusion.2, f32[128,1,8,128]{0,3,2,1:T(8,128)S(1)} %get-tuple-element.238, bf16[2,4096,1,128]{3,1,0,2:T(8,128)(2,1)} %get-tuple-element.255, ...), kind=kOutput, calls=%fused_computation.11.clone.1 | convolution fusion | flops 273022976 | bytes 5513477 | tf_op jit(solution)/shard_map/while/body/eval_jaxpr/bgqpl,plgd->bgqd/dot_general | solution.py:125
  233.4 3.6 %fusion.78 = (f32[128,8]{0,1:T(8,128)S(1)}, f32[2,512,128,8]{2,1,3,0:T(8,128)}) fusion(pred[128,2]{0,1:T(4,128)(4,1)S(1)} %compare_bitcast_fusion.2, bf16[128,1,8,128]{3,0,2,1:T(8,128)(2,1)S(1)} %get-tuple-element.254, bf16[2,4096,1,128]{3,1,0,2:T(8,128)(2,1)} %get-tuple-element.253, s32[]{:T(128)S(6)} %select_n.55), kind=kOutput, calls=%fused_computation.6.clone.1 | convolution fusion | flops 271580160 | bytes 4722948 | tf_op jit(solution)/shard_map/while/body/eval_jaxpr/bgqd,plgd->bgqpl/dot_general | solution.py:115
  237.0 3.6 %fusion.81 = f32[128,1,8,128]{0,3,2,1:T(8,128)S(1)} fusion(f32[2,512,128,8]{2,1,3,0:T(8,128)} %get-tuple-element.220, f32[128,8]{0,1:T(8,128)S(1)} %bitcast.213, pred[128,2]{0,1:T(4,128)(4,1)S(1)} %compare_bitcast_fusion.2, f32[128,1,8,128]{0,3,2,1:T(8,128)S(1)} %get-tuple-element.238, bf16[2,4096,1,128]{3,1,0,2:T(8,128)(2,1)} %get-tuple-element.255, ...), kind=kOutput, calls=%fused_computation.11.clone.1 | convolution fusion | flops 273022976 | bytes 5513477 | tf_op jit(solution)/shard_map/while/body/eval_jaxpr/bgqpl,plgd->bgqd/dot_general | solution.py:125
  242.7 3.6 %fusion.78 = (f32[128,8]{0,1:T(8,128)S(1)}, f32[2,512,128,8]{2,1,3,0:T(8,128)}) fusion(pred[128,2]{0,1:T(4,128)(4,1)S(1)} %compare_bitcast_fusion.2, bf16[128,1,8,128]{3,0,2,1:T(8,128)(2,1)S(1)} %get-tuple-element.254, bf16[2,4096,1,128]{3,1,0,2:T(8,128)(2,1)} %get-tuple-element.253, s32[]{:T(128)S(6)} %select_n.55), kind=kOutput, calls=%fused_computation.6.clone.1 | convolution fusion | flops 271580160 | bytes 4722948 | tf_op jit(solution)/shard_map/while/body/eval_jaxpr/bgqd,plgd->bgqpl/dot_general | solution.py:115
  246.3 3.6 %fusion.81 = f32[128,1,8,128]{0,3,2,1:T(8,128)S(1)} fusion(f32[2,512,128,8]{2,1,3,0:T(8,128)} %get-tuple-element.220, f32[128,8]{0,1:T(8,128)S(1)} %bitcast.213, pred[128,2]{0,1:T(4,128)(4,1)S(1)} %compare_bitcast_fusion.2, f32[128,1,8,128]{0,3,2,1:T(8,128)S(1)} %get-tuple-element.238, bf16[2,4096,1,128]{3,1,0,2:T(8,128)(2,1)} %get-tuple-element.255, ...), kind=kOutput, calls=%fused_computation.11.clone.1 | convolution fusion | flops 273022976 | bytes 5513477 | tf_op jit(solution)/shard_map/while/body/eval_jaxpr/bgqpl,plgd->bgqd/dot_general | solution.py:125
  252.1 3.6 %fusion.78 = (f32[128,8]{0,1:T(8,128)S(1)}, f32[2,512,128,8]{2,1,3,0:T(8,128)}) fusion(pred[128,2]{0,1:T(4,128)(4,1)S(1)} %compare_bitcast_fusion.2, bf16[128,1,8,128]{3,0,2,1:T(8,128)(2,1)S(1)} %get-tuple-element.254, bf16[2,4096,1,128]{3,1,0,2:T(8,128)(2,1)} %get-tuple-element.253, s32[]{:T(128)S(6)} %select_n.55), kind=kOutput, calls=%fused_computation.6.clone.1 | convolution fusion | flops 271580160 | bytes 4722948 | tf_op jit(solution)/shard_map/while/body/eval_jaxpr/bgqd,plgd->bgqpl/dot_general | solution.py:115
  255.7 3.6 %fusion.81 = f32[128,1,8,128]{0,3,2,1:T(8,128)S(1)} fusion(f32[2,512,128,8]{2,1,3,0:T(8,128)} %get-tuple-element.220, f32[128,8]{0,1:T(8,128)S(1)} %bitcast.213, pred[128,2]{0,1:T(4,128)(4,1)S(1)} %compare_bitcast_fusion.2, f32[128,1,8,128]{0,3,2,1:T(8,128)S(1)} %get-tuple-element.238, bf16[2,4096,1,128]{3,1,0,2:T(8,128)(2,1)} %get-tuple-element.255, ...), kind=kOutput, calls=%fused_computation.11.clone.1 | convolution fusion | flops 273022976 | bytes 5513477 | tf_op jit(solution)/shard_map/while/body/eval_jaxpr/bgqpl,plgd->bgqd/dot_general | solution.py:125
  261.5 3.6 %fusion.78 = (f32[128,8]{0,1:T(8,128)S(1)}, f32[2,512,128,8]{2,1,3,0:T(8,128)}) fusion(pred[128,2]{0,1:T(4,128)(4,1)S(1)} %compare_bitcast_fusion.2, bf16[128,1,8,128]{3,0,2,1:T(8,128)(2,1)S(1)} %get-tuple-element.254, bf16[2,4096,1,128]{3,1,0,2:T(8,128)(2,1)} %get-tuple-element.253, s32[]{:T(128)S(6)} %select_n.55), kind=kOutput, calls=%fused_computation.6.clone.1 | convolution fusion | flops 271580160 | bytes 4722948 | tf_op jit(solution)/shard_map/while/body/eval_jaxpr/bgqd,plgd->bgqpl/dot_general | solution.py:115
  265.1 3.6 %fusion.81 = f32[128,1,8,128]{0,3,2,1:T(8,128)S(1)} fusion(f32[2,512,128,8]{2,1,3,0:T(8,128)} %get-tuple-element.220, f32[128,8]{0,1:T(8,128)S(1)} %bitcast.213, pred[128,2]{0,1:T(4,128)(4,1)S(1)} %compare_bitcast_fusion.2, f32[128,1,8,128]{0,3,2,1:T(8,128)S(1)} %get-tuple-element.238, bf16[2,4096,1,128]{3,1,0,2:T(8,128)(2,1)} %get-tuple-element.255, ...), kind=kOutput, calls=%fused_computation.11.clone.1 | convolution fusion | flops 273022976 | bytes 5513477 | tf_op jit(solution)/shard_map/while/body/eval_jaxpr/bgqpl,plgd->bgqd/dot_general | solution.py:125
  270.8 3.6 %fusion.78 = (f32[128,8]{0,1:T(8,128)S(1)}, f32[2,512,128,8]{2,1,3,0:T(8,128)}) fusion(pred[128,2]{0,1:T(4,128)(4,1)S(1)} %compare_bitcast_fusion.2, bf16[128,1,8,128]{3,0,2,1:T(8,128)(2,1)S(1)} %get-tuple-element.254, bf16[2,4096,1,128]{3,1,0,2:T(8,128)(2,1)} %get-tuple-element.253, s32[]{:T(128)S(6)} %select_n.55), kind=kOutput, calls=%fused_computation.6.clone.1 | convolution fusion | flops 271580160 | bytes 4722948 | tf_op jit(solution)/shard_map/while/body/eval_jaxpr/bgqd,plgd->bgqpl/dot_general | solution.py:115
  274.4 3.6 %fusion.81 = f32[128,1,8,128]{0,3,2,1:T(8,128)S(1)} fusion(f32[2,512,128,8]{2,1,3,0:T(8,128)} %get-tuple-element.220, f32[128,8]{0,1:T(8,128)S(1)} %bitcast.213, pred[128,2]{0,1:T(4,128)(4,1)S(1)} %compare_bitcast_fusion.2, f32[128,1,8,128]{0,3,2,1:T(8,128)S(1)} %get-tuple-element.238, bf16[2,4096,1,128]{3,1,0,2:T(8,128)(2,1)} %get-tuple-element.255, ...), kind=kOutput, calls=%fused_computation.11.clone.1 | convolution fusion | flops 273022976 | bytes 5513477 | tf_op jit(solution)/shard_map/while/body/eval_jaxpr/bgqpl,plgd->bgqd/dot_general | solution.py:125
  280.2 3.6 %fusion.78 = (f32[128,8]{0,1:T(8,128)S(1)}, f32[2,512,128,8]{2,1,3,0:T(8,128)}) fusion(pred[128,2]{0,1:T(4,128)(4,1)S(1)} %compare_bitcast_fusion.2, bf16[128,1,8,128]{3,0,2,1:T(8,128)(2,1)S(1)} %get-tuple-element.254, bf16[2,4096,1,128]{3,1,0,2:T(8,128)(2,1)} %get-tuple-element.253, s32[]{:T(128)S(6)} %select_n.55), kind=kOutput, calls=%fused_computation.6.clone.1 | convolution fusion | flops 271580160 | bytes 4722948 | tf_op jit(solution)/shard_map/while/body/eval_jaxpr/bgqd,plgd->bgqpl/dot_general | solution.py:115
  283.8 3.6 %fusion.81 = f32[128,1,8,128]{0,3,2,1:T(8,128)S(1)} fusion(f32[2,512,128,8]{2,1,3,0:T(8,128)} %get-tuple-element.220, f32[128,8]{0,1:T(8,128)S(1)} %bitcast.213, pred[128,2]{0,1:T(4,128)(4,1)S(1)} %compare_bitcast_fusion.2, f32[128,1,8,128]{0,3,2,1:T(8,128)S(1)} %get-tuple-element.238, bf16[2,4096,1,128]{3,1,0,2:T(8,128)(2,1)} %get-tuple-element.255, ...), kind=kOutput, calls=%fused_computation.11.clone.1 | convolution fusion | flops 273022976 | bytes 5513477 | tf_op jit(solution)/shard_map/while/body/eval_jaxpr/bgqpl,plgd->bgqd/dot_general | solution.py:125
  289.5 3.6 %fusion.78 = (f32[128,8]{0,1:T(8,128)S(1)}, f32[2,512,128,8]{2,1,3,0:T(8,128)}) fusion(pred[128,2]{0,1:T(4,128)(4,1)S(1)} %compare_bitcast_fusion.2, bf16[128,1,8,128]{3,0,2,1:T(8,128)(2,1)S(1)} %get-tuple-element.254, bf16[2,4096,1,128]{3,1,0,2:T(8,128)(2,1)} %get-tuple-element.253, s32[]{:T(128)S(6)} %select_n.55), kind=kOutput, calls=%fused_computation.6.clone.1 | convolution fusion | flops 271580160 | bytes 4722948 | tf_op jit(solution)/shard_map/while/body/eval_jaxpr/bgqd,plgd->bgqpl/dot_general | solution.py:115
  293.2 3.6 %fusion.81 = f32[128,1,8,128]{0,3,2,1:T(8,128)S(1)} fusion(f32[2,512,128,8]{2,1,3,0:T(8,128)} %get-tuple-element.220, f32[128,8]{0,1:T(8,128)S(1)} %bitcast.213, pred[128,2]{0,1:T(4,128)(4,1)S(1)} %compare_bitcast_fusion.2, f32[128,1,8,128]{0,3,2,1:T(8,128)S(1)} %get-tuple-element.238, bf16[2,4096,1,128]{3,1,0,2:T(8,128)(2,1)} %get-tuple-element.255, ...), kind=kOutput, calls=%fused_computation.11.clone.1 | convolution fusion | flops 273022976 | bytes 5513477 | tf_op jit(solution)/shard_map/while/body/eval_jaxpr/bgqpl,plgd->bgqd/dot_general | solution.py:125
  (144 shorter events, 34.1 us)
Async XLA Ops:
  7.2 19.6 %copy-start.6 = (s32[32]{0:T(128)S(1)}, s32[32]{0:T(128)}, u32[]{:S(2)}) copy-start(s32[32]{0:T(128)} %param.20) | copy-start | bytes 388
  7.2 19.8 %copy-start.3 = (bf16[8192]{0:T(1024)(128)(2,1)S(1)}, bf16[8192]{0:T(1024)(128)(2,1)}, u32[]{:S(2)}) copy-start(bf16[8192]{0:T(1024)(128)(2,1)} %param.13) | copy-start | bytes 49156
  7.2 138.5 %all-gather.5.cloned.1.call-start = ((), (), s32[]{:S(2)}) async-start(), calls=%async_computation.2 | async-start | bytes 21299200 | tf_op jit(solution)/shard_map/all_gather | solution.py:83
  9.8 20.7 %copy-start.4 = (bf16[1024]{0:T(1024)(128)(2,1)S(1)}, bf16[1024]{0:T(1024)(128)(2,1)}, u32[]{:S(2)}) copy-start(bf16[1024]{0:T(1024)(128)(2,1)} %param.15) | copy-start | bytes 6148
  9.8 20.7 %copy-start.5 = (s32[32]{0:T(128)S(1)}, s32[32]{0:T(128)}, u32[]{:S(2)}) copy-start(s32[32]{0:T(128)} %param.21) | copy-start | bytes 388
  9.9 21.2 %copy-start.1 = (bf16[128,8192]{1,0:T(8,128)(2,1)S(1)}, bf16[128,8192]{1,0:T(8,128)(2,1)}, u32[]{:S(2)}) copy-start(bf16[128,8192]{1,0:T(8,128)(2,1)} %param.12) | copy-start | bytes 6291460
  12.6 19.0 %copy-start.7 = (bf16[2,128]{1,0:T(2,128)(2,1)S(1)}, bf16[2,128]{1,0:T(2,128)(2,1)}, u32[]{:S(2)}) copy-start(bf16[2,128]{1,0:T(2,128)(2,1)} %param.17) | copy-start | bytes 1540
  12.6 76.7 %all-to-all-start = ((bf16[64,2,64,1,128]{4,2,1,3,0:T(8,128)(2,1)}), bf16[64,2,64,1,128]{4,2,1,3,0:T(8,128)(2,1)}, u32[]{:S(2)}, u32[]{:S(2)}) async-start(bf16[64,2,64,1,128]{4,2,1,3,0:T(8,128)(2,1)} %stack.2), calls=%async_computation | async-start | bytes 4194304 | tf_op jit(solution)/shard_map/all_to_all | solution.py:106
  25.9 196.8 %all-gather.3.cloned.1.call-start = ((), (), s32[]{:S(2)}) async-start(), calls=%async_computation.1 | async-start | bytes 2129920 | tf_op jit(solution)/shard_map/all_gather | solution.py:104
  155.8 142.7 %copy-start.2 = (bf16[128,128]{1,0:T(8,128)(2,1)}, bf16[128,128]{1,0:T(8,128)(2,1)S(1)}, u32[]{:S(2)}) copy-start(bf16[128,128]{1,0:T(8,128)(2,1)S(1)} %get-tuple-element.148) | copy-start | bytes 98308
  155.9 142.6 %collective-permute-start = (bf16[128,256]{1,0:T(8,128)(2,1)S(1)}, bf16[128,256]{1,0:T(8,128)(2,1)S(1)}, u32[]{:S(2)}, u32[]{:S(2)}) collective-permute-start(bf16[128,256]{1,0:T(8,128)(2,1)S(1)} %pad_maximum_fusion.3), channel_id=1, source_target_pairs={{0,12},{4,16},{8,20},{12,24},{16,28},{20,32},{24,36},{28,40},{32,4... | collective-permute-start | bytes 196616 | tf_op jit(solution)/shard_map/ppermute | solution.py:14
  158.3 140.1 %collective-permute-start.1 = (bf16[128,256]{1,0:T(8,128)(2,1)S(1)}, bf16[128,256]{1,0:T(8,128)(2,1)}, u32[]{:S(2)}, u32[]{:S(2)}) collective-permute-start(bf16[128,256]{1,0:T(8,128)(2,1)S(1)} %pad_maximum_fusion.3), channel_id=1, source_target_pairs={{0,8},{4,12},{8,16},{12,20},{16,24},{20,28},{24,32},{28,36},{32,40... | collective-permute-start | bytes 196616 | tf_op jit(solution)/shard_map/ppermute | solution.py:14
  163.4 135.1 %collective-permute-start.2 = (bf16[128,256]{1,0:T(8,128)(2,1)S(1)}, bf16[128,256]{1,0:T(8,128)(2,1)}, u32[]{:S(2)}, u32[]{:S(2)}) collective-permute-start(bf16[128,256]{1,0:T(8,128)(2,1)S(1)} %pad_maximum_fusion.3), channel_id=1, source_target_pairs={{0,4},{4,8},{8,12},{12,16},{16,20},{20,24},{24,28},{28,32},{32,36}... | collective-permute-start | bytes 196616 | tf_op jit(solution)/shard_map/ppermute | solution.py:14
  227.6 3.6 %copy-start = (f32[2,512,128,8]{2,1,3,0:T(8,128)S(1)}, f32[2,512,128,8]{2,1,3,0:T(8,128)}, u32[]{:S(2)}) copy-start(f32[2,512,128,8]{2,1,3,0:T(8,128)} %get-tuple-element.220) | copy-start | bytes 12582916 | tf_op jit(solution)/shard_map/while
  237.0 3.6 %copy-start = (f32[2,512,128,8]{2,1,3,0:T(8,128)S(1)}, f32[2,512,128,8]{2,1,3,0:T(8,128)}, u32[]{:S(2)}) copy-start(f32[2,512,128,8]{2,1,3,0:T(8,128)} %get-tuple-element.220) | copy-start | bytes 12582916 | tf_op jit(solution)/shard_map/while
  246.3 3.6 %copy-start = (f32[2,512,128,8]{2,1,3,0:T(8,128)S(1)}, f32[2,512,128,8]{2,1,3,0:T(8,128)}, u32[]{:S(2)}) copy-start(f32[2,512,128,8]{2,1,3,0:T(8,128)} %get-tuple-element.220) | copy-start | bytes 12582916 | tf_op jit(solution)/shard_map/while
  255.7 3.6 %copy-start = (f32[2,512,128,8]{2,1,3,0:T(8,128)S(1)}, f32[2,512,128,8]{2,1,3,0:T(8,128)}, u32[]{:S(2)}) copy-start(f32[2,512,128,8]{2,1,3,0:T(8,128)} %get-tuple-element.220) | copy-start | bytes 12582916 | tf_op jit(solution)/shard_map/while
  265.1 3.6 %copy-start = (f32[2,512,128,8]{2,1,3,0:T(8,128)S(1)}, f32[2,512,128,8]{2,1,3,0:T(8,128)}, u32[]{:S(2)}) copy-start(f32[2,512,128,8]{2,1,3,0:T(8,128)} %get-tuple-element.220) | copy-start | bytes 12582916 | tf_op jit(solution)/shard_map/while
  274.4 3.6 %copy-start = (f32[2,512,128,8]{2,1,3,0:T(8,128)S(1)}, f32[2,512,128,8]{2,1,3,0:T(8,128)}, u32[]{:S(2)}) copy-start(f32[2,512,128,8]{2,1,3,0:T(8,128)} %get-tuple-element.220) | copy-start | bytes 12582916 | tf_op jit(solution)/shard_map/while
  283.8 3.6 %copy-start = (f32[2,512,128,8]{2,1,3,0:T(8,128)S(1)}, f32[2,512,128,8]{2,1,3,0:T(8,128)}, u32[]{:S(2)}) copy-start(f32[2,512,128,8]{2,1,3,0:T(8,128)} %get-tuple-element.220) | copy-start | bytes 12582916 | tf_op jit(solution)/shard_map/while
  293.1 3.6 %copy-start = (f32[2,512,128,8]{2,1,3,0:T(8,128)S(1)}, f32[2,512,128,8]{2,1,3,0:T(8,128)}, u32[]{:S(2)}) copy-start(f32[2,512,128,8]{2,1,3,0:T(8,128)} %get-tuple-element.220) | copy-start | bytes 12582916 | tf_op jit(solution)/shard_map/while
Sparse Core Ops, SparseCore 0:
  10.7 134.8 all-gather.4
  148.4 74.2 all-gather.2
